TPU v7x, 32 devices: a whole 2x2x4 slice. The times are simulated.
32 devices in a mesh: groups: 2 (over x), wide: 4 (over y, core), expert: 4 (over z).
Axes of the slice: x: 2, y: 2, z: 4, core: 2. Of those that a mesh axis runs over, the one named last changes fastest.
Arguments:
- prompts: bfloat16 [8, 128, 6144], P(('groups', 'wide'), None, 'expert'), parts along dimension 0, may hold values from -6 to 6
- span_slot_owner: int32 [8], P('groups'), parts along dimension 0, may hold values from 0 to 3, as said below
- row_expert_index: int32 [768, 2], P('groups'), parts along dimension 0, may hold values from 0 to 7, all different within a row
- tile_tenant_index: int32 [6], P('groups'), parts along dimension 0, may hold values from 0 to 7
- tenant_adapter_slot: int32 [16], P('groups'), parts along dimension 0, may hold values from 0 to 7, each once
- router: bfloat16 [6144, 8], replicated, may hold values from -0.078125 to 0.078125
- gate_weight: bfloat16 [2, 6144, 16384], P(None, None, ('wide', 'expert')), may hold values from -0.078125 to 0.078125
- up_weight: bfloat16 [2, 6144, 16384], P(None, None, ('wide', 'expert')), may hold values from -0.078125 to 0.078125
- down_weight: bfloat16 [2, 16384, 6144], P(None, 'wide', 'expert'), may hold values from -0.046875 to 0.046875
- adapter_down_weight: bfloat16 [16, 2, 6144, 64], P(('groups', 'wide'), None, 'expert'), parts along dimension 0, may hold values from -0.078125 to 0.078125
- adapter_up_weight: bfloat16 [16, 2, 64, 16384], P('groups', None, None, ('wide', 'expert')), parts along dimension 0, may hold values from -0.75 to 0.75
Outputs:
- mixed: bfloat16 [768, 6144], P(('groups', 'wide'), 'expert'), parts along dimension 0
There are 2 independent parts, one for each index of `groups`. A program takes and returns all parts, laid end to end along the dimension named above; an argument that names none is the same for every part. Nothing has to cross between parts.
Inputs may be any that keep to these rules, and one draw needn't show every extreme that they name: `span_slot_owner`: a permutation of the slots; span c, for c < 3, is in slot span_slot_owner[c]. `row_expert_index`: each row names two different experts. `tenant_adapter_slot`: a permutation of the slots. `tile_tenant_index`: tenant of rows 128 * i to 128 * i + 127.
All inputs are finite; a program needn't handle non-finite values.
Results may differ from a plain program's by a relative error of at most 0.0051.
Values may be sent and summed in bfloat16 or wider, within the bound.
No kernel may reach another device: no remote copies, remote signals or barrier semaphores. Data moves between devices by JAX's collectives and lax.ppermute only.
A program may use at most 128 MiB of HBM per device.

v0:
```python
import jax
import jax.numpy as jnp
import numpy as np
from jax import lax
from jax.sharding import Mesh
from jax.sharding import PartitionSpec as P

ADAPTER_SCALE = 0.5
WIDE = ("wy", "wc")
GROUP = ("wy", "wc", "expert")


def per_device(
    prompts,
    span_slot_owner,
    row_expert_index,
    tile_tenant_index,
    tenant_adapter_slot,
    router,
    gate_weight,
    up_weight,
    down_weight,
    adapter_down_weight,
    adapter_up_weight,
):
    span = prompts.shape[1]
    quarter = prompts.shape[2]
    tokens = row_expert_index.shape[0]
    nchunk = tokens // span
    window = gate_weight.shape[0]
    core = lax.axis_index("wc")
    cores = lax.axis_size("wc")
    wide_index = lax.axis_index(WIDE)
    tile_count = tile_tenant_index.shape[0]
    tile_rows = tokens // tile_count
    resident_slots = adapter_down_weight.shape[0]
    rank = adapter_down_weight.shape[3]
    slot_of_span = span_slot_owner[:nchunk]
    held_slots = prompts.shape[0]
    if lax.axis_size("wy") == 2 and cores == 2:
        pair = [(0, 1), (1, 0)]
        slot_chip = lax.ppermute(prompts, "wy", pair)
        slot_core = lax.ppermute(prompts, "wc", pair)
        slot_both = lax.ppermute(slot_chip, "wc", pair)
        slots_q = jnp.concatenate([prompts, slot_core, slot_chip, slot_both], axis=0)
        slot_pick = (
            jnp.bitwise_xor(slot_of_span // held_slots, wide_index) * held_slots
            + slot_of_span % held_slots
        )
    else:
        slots_q = lax.all_gather(prompts, WIDE, axis=0, tiled=True)
        slot_pick = slot_of_span
    rows_q = jnp.take(slots_q, slot_pick, axis=0).reshape(tokens, quarter)
    chips = lax.axis_size("wy")
    tile_slot_index = jnp.take(tenant_adapter_slot, tile_tenant_index)
    holder = tile_slot_index // resident_slots
    local_slot = tile_slot_index % resident_slots
    if chips == 2 and cores == 2:
        swap = [(0, 1), (1, 0)]
        from_chip = lax.ppermute(adapter_down_weight, "wy", swap)
        from_core = lax.ppermute(adapter_down_weight, "wc", swap)
        from_both = lax.ppermute(from_chip, "wc", swap)
        stacked = jnp.stack([adapter_down_weight, from_core, from_chip, from_both])
        source = jnp.bitwise_xor(holder, wide_index)
    else:
        stacked = lax.all_gather(adapter_down_weight, WIDE, axis=0, tiled=False)
        source = holder
    flat_held = stacked.reshape((-1,) + adapter_down_weight.shape[1:])
    tile_adapters = jnp.take(flat_held, source * resident_slots + local_slot, axis=0)
    partial_rank = jnp.einsum(
        "ntd,nedr->nter",
        rows_q.reshape(tile_count, tile_rows, quarter),
        tile_adapters,
        preferred_element_type=jnp.float32,
    ).reshape(tokens, window * rank)
    rank_top = lax.reduce_precision(partial_rank, exponent_bits=8, mantissa_bits=7)
    rank_hi = rank_top.astype(jnp.bfloat16)
    rank_lo = (partial_rank - rank_top).astype(jnp.bfloat16)
    half = tokens // cores
    expert_size = lax.axis_size("expert")
    swap = [(i, (i + 1) % cores) for i in range(cores)]
    mine_q = lax.dynamic_slice_in_dim(rows_q, core * half, half, 0)
    mine = lax.all_gather(mine_q, "expert", axis=1, tiled=True)
    rank_q = lax.dynamic_slice_in_dim(
        jnp.concatenate([rank_hi, rank_lo], axis=1), core * half, half, 0
    )
    rank_q, _ = lax.optimization_barrier((rank_q, mine))
    pieces = lax.all_gather(rank_q, "expert", axis=1, tiled=False).astype(jnp.float32)
    mine_rank = jnp.sum(pieces[:, :, : window * rank] + pieces[:, :, window * rank :], axis=1)
    mine_rank = mine_rank.astype(jnp.bfloat16)
    other = lax.ppermute(mine, "wc", swap)
    other_rank = lax.ppermute(mine_rank, "wc", swap)
    input_rows = jnp.where(
        core == 0, jnp.concatenate([mine, other], axis=0), jnp.concatenate([other, mine], axis=0)
    )
    input_rows = lax.optimization_barrier(input_rows)
    lowrank = jnp.where(
        core == 0,
        jnp.concatenate([mine_rank, other_rank], axis=0),
        jnp.concatenate([other_rank, mine_rank], axis=0),
    ).reshape(tile_count, tile_rows, window, rank)
    logits = jnp.dot(input_rows, router, preferred_element_type=jnp.float32)
    experts = jnp.arange(router.shape[1], dtype=jnp.int32)
    picked = (row_expert_index[:, :, None] == experts[None, None, :]).astype(jnp.float32)
    chosen = jnp.sum(picked * logits[:, None, :], axis=2)
    first_prob = jax.nn.sigmoid(chosen[:, 0] - chosen[:, 1])
    second_prob = jax.nn.sigmoid(chosen[:, 1] - chosen[:, 0])
    weight = (
        first_prob[:, None] * picked[:, 0, :window] + second_prob[:, None] * picked[:, 1, :window]
    )
    tile_up = jnp.take(adapter_up_weight, tile_tenant_index, axis=0)
    adapted_hidden = jnp.einsum(
        "nter,nerf->ntef", lowrank, tile_up, preferred_element_type=jnp.float32
    ).reshape(tokens, window, tile_up.shape[3])
    running = None
    for expert_number in range(window):
        gate_pre = jnp.dot(
            input_rows, gate_weight[expert_number], preferred_element_type=jnp.float32
        )
        up_value = (
            jnp.dot(input_rows, up_weight[expert_number], preferred_element_type=jnp.float32)
            + ADAPTER_SCALE * adapted_hidden[:, expert_number]
        )
        hidden = (weight[:, expert_number, None] * jax.nn.silu(gate_pre) * up_value).astype(
            jnp.bfloat16
        )
        gathered = lax.all_gather(hidden, "expert", axis=1, tiled=True)
        part = jnp.dot(gathered, down_weight[expert_number], preferred_element_type=jnp.float32)
        running = part if running is None else running + part
    return reduce_rows(running, core, cores).astype(jnp.bfloat16)


def reduce_rows(running, core, cores):
    chips = lax.axis_size("wy")
    block = running.shape[0] // (chips * cores)
    by_chip = running.reshape(chips, cores, block, running.shape[1])
    keep = jnp.where(core == 0, by_chip[:, 0], by_chip[:, 1])
    send = jnp.where(core == 0, by_chip[:, 1], by_chip[:, 0])
    chip_sum = keep + lax.ppermute(send, "wc", [(i, (i + 1) % cores) for i in range(cores)])
    if chips == 2:
        chip = lax.axis_index("wy")
        mine = jnp.where(chip == 0, chip_sum[0], chip_sum[1])
        away = jnp.where(chip == 0, chip_sum[1], chip_sum[0])
        arrived = lax.ppermute(away.astype(jnp.bfloat16), "wy", [(0, 1), (1, 0)])
        return mine + arrived.astype(jnp.float32)
    return lax.psum_scatter(chip_sum, "wy", scatter_dimension=0, tiled=True).reshape(block, -1)


def solution(mesh):
    groups = mesh.shape["groups"]
    wide = mesh.shape["wide"]
    expert = mesh.shape["expert"]
    split = Mesh(
        np.asarray(mesh.devices).reshape(groups, wide // 2, 2, expert),
        ("groups", "wy", "wc", "expert"),
    )
    rows = ("groups", "wy", "wc")
    in_specs = (
        P(rows, None, "expert"),
        P("groups"),
        P("groups", None),
        P("groups"),
        P("groups"),
        P(),
        P(None, None, GROUP),
        P(None, None, GROUP),
        P(None, WIDE, "expert"),
        P(rows, None, "expert", None),
        P("groups", None, None, GROUP),
    )
    out_specs = P(rows, "expert")
    return jax.shard_map(
        per_device, mesh=split, in_specs=in_specs, out_specs=out_specs, check_vma=False
    )
```

profile of v0, /device:TPU:0, one launch (start us, length us, event | category | flops | bytes accessed | tf_op | source)
XLA Modules:
  0.0 282.4 jit_solution(12810220067142073298)
XLA Ops:
  6.5 3.0 %collective-permute-start.1 = (bf16[1,128,1536]{2,1,0:T(8,128)(2,1)}, bf16[1,128,1536]{2,1,0:T(8,128)(2,1)S(1)}, u32[]{:S(2)}, u32[]{:S(2)}) collective-permute-start(bf16[1,128,1536]{2,1,0:T(8,128)(2,1)} %param.11), channel_id=1, source_target_pairs={{0,8},{8,0},{1,9},{9,1},{2,10},{10,2},{3,11},{11,3},{4,12},{12,4},... | collective-permute-start | bytes 1179656 | tf_op jit(solution)/shard_map/ppermute | solution.py:42
  9.5 9.3 %collective-permute-done.1 = bf16[1,128,1536]{2,1,0:T(8,128)(2,1)S(1)} collective-permute-done((bf16[1,128,1536]{2,1,0:T(8,128)(2,1)}, bf16[1,128,1536]{2,1,0:T(8,128)(2,1)S(1)}, u32[]{:S(2)}, u32[]{:S(2)}) %collective-permute-start.1) | collective-permute-done | bytes 393248 | tf_op jit(solution)/shard_map/ppermute | solution.py:42
  18.8 0.7 compare_and_fusion.2
  19.5 0.1 broadcast_bitcast_fusion
  19.6 0.1 dynamic-slice
  19.7 0.9 collective-permute-done.2
  20.6 2.4 pad_maximum_fusion.1
  22.9 2.1 gather_fusion
  25.0 1.2 dynamic-slice_select_fusion
  26.3 1.8 collective-permute-start.5
  28.1 18.2 %collective-permute-done.5 = bf16[2,2,1536,64]{2,3,1,0:T(8,128)(2,1)} collective-permute-done((bf16[2,2,1536,64]{2,3,1,0:T(8,128)(2,1)}, bf16[2,2,1536,64]{2,3,1,0:T(8,128)(2,1)}, u32[]{:S(2)}, u32[]{:S(2)}) %collective-permute-start.5) | collective-permute-done | bytes 786464 | tf_op jit(solution)/shard_map/ppermute | solution.py:60
  46.3 0.6 gather_fusion.2
  47.0 1.9 collective-permute-done.6
  48.9 3.2 %pad_maximum_fusion = bf16[4,2,2,1536,64]{3,4,2,1,0:T(8,128)(2,1)} fusion(bf16[1,2,2,1536,64]{3,4,2,1,0:T(8,128)(2,1)} %bitcast.9, bf16[1,2,2,1536,64]{3,4,2,1,0:T(8,128)(2,1)} %bitcast.8, bf16[1,2,2,1536,64]{3,4,2,1,0:T(8,128)(2,1)} %bitcast.7, bf16[1,2,2,1536,64]{3,4,2,1,0:T(8,128)(2,1)} %bitcast.119), kind=kLoop, calls=%fused_computation.23 | loop fusion | flops 4718592 | bytes 6291456 | tf_op jit(solution)/shard_map/stack | solution.py:63
  52.1 2.5 gather_fusion.3
  54.6 23.7 %all-gather.5.cloned.1.call-done = bf16[192,6144]{1,0:T(8,128)(2,1)} async-done(((bf16[192,1536]{1,0:T(8,128)(2,1)}), bf16[192,6144]{1,0:T(8,128)(2,1)}) %all-gather.5.cloned.1.call-update) | async-done | bytes 2359312 | tf_op jit(solution)/shard_map/all_gather | solution.py:83
  78.3 0.2 broadcast_select_fusion
  78.5 1.1 copy-done.9
  79.6 0.5 fusion.33
  80.1 0.1 copy.18
  80.3 0.2 fusion.44
  80.5 15.9 %all-gather = bf16[192,1024]{0,1:T(8,128)(2,1)S(1)} all-gather(bf16[192,256]{0,1:T(8,128)(2,1)S(1)} %fusion.44), channel_id=2, replica_groups=mesh['groups'=2,'wy'=2,'wc'=2,'expert'=4] {'expert'}, dimensions={1}, use_global_device_ids=true | all-gather | bytes 491520 | tf_op jit(solution)/shard_map/all_gather | solution.py:88
  96.4 0.1 bitcast_convert_fusion
  96.6 0.1 collective-permute-start.7
  96.7 0.6 gather_fusion.1
  97.3 0.6 collective-permute-done.7
  97.9 0.1 maximum_select_fusion.1
  98.1 0.6 convolution_bitcast_fusion
  98.7 0.2 copy.20
  99.0 2.5 copy-done.10
  101.5 4.0 %maximum_select_fusion = bf16[384,6144]{1,0:T(8,128)(2,1)S(1)} fusion(bf16[192,6144]{1,0:T(8,128)(2,1)} %collective-permute-done.3, bf16[192,6144]{1,0:T(8,128)(2,1)S(1)} %copy-done.10, pred[]{:T(512)S(6)} %eq.14), kind=kLoop, calls=%fused_computation.22 | loop fusion | flops 21233664 | bytes 9437185 | tf_op jit(solution)/shard_map/jit(_where)/select_n | solution.py:93
  105.5 1.3 fusion.53
  107.0 8.1 %fusion.4 = f32[384,1024]{1,0:T(8,128)S(1)} fusion(bf16[384,6144]{1,0:T(8,128)(2,1)S(1)} %maximum_select_fusion, bf16[2,6144,1024]{2,1,0:T(8,128)(2,1)} %param.17), kind=kOutput, calls=%fused_computation.8 | convolution fusion | flops 4831838208 | bytes 18874368 | tf_op jit(solution)/shard_map/dot_general | solution.py:117
  115.1 9.0 %fusion.24 = bf16[384,1024]{1,0:T(8,128)(2,1)} fusion(f32[384,2,1024]{2,0,1:T(8,128)S(1)} %bitcast.114, f32[384,1024]{1,0:T(8,128)S(1)} %fusion.4, bf16[384,6144]{1,0:T(8,128)(2,1)S(1)} %maximum_select_fusion, bf16[2,6144,1024]{2,1,0:T(8,128)(2,1)} %param.18, f32[384]{0:T(512)S(1)} %get-tuple-element.8), kind=kOutput, calls=%fused_computation.30 | convolution fusion | flops 4835377152 | bytes 21235200 | tf_op jit(solution)/shard_map/dot_general | solution.py:121
  124.1 0.2 all-gather.7.cloned.1.call-start
  124.4 11.1 %fusion.10 = f32[384,1024]{1,0:T(8,128)S(1)} fusion(bf16[384,6144]{1,0:T(8,128)(2,1)} %copy-done.3, bf16[2,6144,1024]{2,1,0:T(8,128)(2,1)} %param.17), kind=kOutput, calls=%fused_computation.14 | convolution fusion | flops 4831838208 | bytes 18874368 | tf_op jit(solution)/shard_map/dot_general | solution.py:117
  135.5 9.1 %fusion.28 = bf16[384,1024]{1,0:T(8,128)(2,1)} fusion(f32[384,2,1024]{2,0,1:T(8,128)S(1)} %bitcast.115, f32[384,1024]{1,0:T(8,128)S(1)} %fusion.10, bf16[384,6144]{1,0:T(8,128)(2,1)S(1)} %copy-done.4, bf16[2,6144,1024]{2,1,0:T(8,128)(2,1)} %param.18, f32[384]{0:T(512)S(1)} %get-tuple-element.7), kind=kOutput, calls=%fused_computation.35 | convolution fusion | flops 4835377152 | bytes 21235200 | tf_op jit(solution)/shard_map/dot_general | solution.py:121
  144.6 41.7 %all-gather.9.cloned.1.call-done = bf16[384,4096]{1,0:T(8,128)(2,1)} async-done(((bf16[384,1024]{1,0:T(8,128)(2,1)}), bf16[384,4096]{1,0:T(8,128)(2,1)}) %all-gather.9.cloned.1.call-update) | async-done | bytes 3145744 | tf_op jit(solution)/shard_map/all_gather | solution.py:127
  186.3 10.0 %fusion = f32[384,1536]{1,0:T(8,128)} fusion(bf16[384,4096]{1,0:T(8,128)(2,1)} %all-gather.9.cloned.1.call-done, bf16[2,4096,1536]{2,1,0:T(8,128)(2,1)} %param.19), kind=kOutput, calls=%fused_computation.4 | convolution fusion | flops 4831838208 | bytes 18087936 | tf_op jit(solution)/shard_map/dot_general | solution.py:128
  196.4 53.7 %all-gather.7.cloned.1.call-done = bf16[384,4096]{1,0:T(8,128)(2,1)} async-done(((bf16[384,1024]{1,0:T(8,128)(2,1)}), bf16[384,4096]{1,0:T(8,128)(2,1)}) %all-gather.7.cloned.1.call-update) | async-done | bytes 3145744 | tf_op jit(solution)/shard_map/all_gather | solution.py:127
  250.1 9.3 %fusion.18 = f32[384,1536]{1,0:T(8,128)S(1)} fusion(f32[384,1536]{1,0:T(8,128)} %fusion, bf16[384,4096]{1,0:T(8,128)(2,1)} %all-gather.7.cloned.1.call-done, bf16[2,4096,1536]{2,1,0:T(8,128)(2,1)} %param.19), kind=kOutput, calls=%fused_computation.24 | convolution fusion | flops 4832428032 | bytes 20447232 | tf_op jit(solution)/shard_map/dot_general | solution.py:128
  259.4 1.4 copy-done.5
  260.8 0.1 select_bitcast_fusion
  261.0 2.8 %collective-permute-done.8 = f32[2,96,1536]{2,1,0:T(8,128)S(1)} collective-permute-done((f32[2,96,1536]{2,1,0:T(8,128)S(1)}, f32[2,96,1536]{2,1,0:T(8,128)S(1)}, u32[]{:S(2)}, u32[]{:S(2)}) %collective-permute-start.8) | collective-permute-done | bytes 1179680 | tf_op jit(solution)/shard_map/ppermute | solution.py:139
  263.8 2.0 bitcast_add_fusion
  265.9 1.5 collective-permute-start.9
  267.5 7.6 %collective-permute-done.9 = bf16[96,1536]{1,0:T(8,128)(2,1)S(1)} collective-permute-done((bf16[96,1536]{1,0:T(8,128)(2,1)S(1)}, bf16[96,1536]{1,0:T(8,128)(2,1)S(1)}, u32[]{:S(2)}, u32[]{:S(2)}) %collective-permute-start.9) | collective-permute-done | bytes 294944 | tf_op jit(solution)/shard_map/ppermute | solution.py:144
  275.1 0.8 fusion.38
  (53 shorter events, 0.6 us)
Async XLA Ops:
  6.5 90.2 %copy-start = (bf16[8,2,64,1024]{3,2,1,0:T(8,128)(2,1)S(1)}, bf16[8,2,64,1024]{3,2,1,0:T(8,128)(2,1)}, u32[]{:S(2)}) copy-start(bf16[8,2,64,1024]{3,2,1,0:T(8,128)(2,1)} %param.21) | copy-start | bytes 6291460
  6.5 71.8 %all-gather.5.cloned.1.call-start = ((), (), s32[]{:S(2)}) async-start(), calls=%async_computation | async-start | bytes 2949120 | tf_op jit(solution)/shard_map/all_gather | solution.py:83
  6.5 12.3 %collective-permute-start.1 = (bf16[1,128,1536]{2,1,0:T(8,128)(2,1)}, bf16[1,128,1536]{2,1,0:T(8,128)(2,1)S(1)}, u32[]{:S(2)}, u32[]{:S(2)}) collective-permute-start(bf16[1,128,1536]{2,1,0:T(8,128)(2,1)} %param.11), channel_id=1, source_target_pairs={{0,8},{8,0},{1,9},{9,1},{2,10},{10,2},{3,11},{11,3},{4,12},{12,4},... | collective-permute-start | bytes 1179656 | tf_op jit(solution)/shard_map/ppermute | solution.py:42
  9.5 10.2 %collective-permute-start = (bf16[1,128,1536]{2,1,0:T(8,128)(2,1)}, bf16[1,128,1536]{2,1,0:T(8,128)(2,1)S(1)}, u32[]{:S(2)}, u32[]{:S(2)}) collective-permute-start(bf16[1,128,1536]{2,1,0:T(8,128)(2,1)} %param.11), channel_id=1, source_target_pairs={{0,4},{4,0},{1,5},{5,1},{2,6},{6,2},{3,7},{7,3},{8,12},{12,8},{9,1... | collective-permute-start | bytes 1179656 | tf_op jit(solution)/shard_map/ppermute | solution.py:43
  18.8 1.7 collective-permute-start.2
  22.9 23.3 %copy-start.13 = (s32[3]{0:T(128)S(1)}, s32[3]{0:T(128)}, u32[]{:S(2)}) copy-start(s32[3]{0:T(128)} %param.14) | copy-start | bytes 40
  22.9 23.3 %copy-start.2 = (s32[8]{0:T(128)S(1)}, s32[8]{0:T(128)}, u32[]{:S(2)}) copy-start(s32[8]{0:T(128)} %param.15) | copy-start | bytes 100
  25.0 27.1 %copy-start.8 = (bf16[3,128,1536]{2,1,0:T(8,128)(2,1)}, bf16[3,128,1536]{2,1,0:T(8,128)(2,1)S(1)}, u32[]{:S(2)}) copy-start(bf16[3,128,1536]{2,1,0:T(8,128)(2,1)S(1)} %gather_fusion) | copy-start | bytes 3538948
  26.2 160.1 %all-gather.9.cloned.1.call-start = ((), (), s32[]{:S(2)}) async-start(), calls=%async_computation.2 | async-start | bytes 3932160 | tf_op jit(solution)/shard_map/all_gather | solution.py:127
  26.3 20.0 %collective-permute-start.5 = (bf16[2,2,1536,64]{2,3,1,0:T(8,128)(2,1)}, bf16[2,2,1536,64]{2,3,1,0:T(8,128)(2,1)}, u32[]{:S(2)}, u32[]{:S(2)}) collective-permute-start(bf16[2,2,1536,64]{2,3,1,0:T(8,128)(2,1)} %param.20), channel_id=1, source_target_pairs={{0,8},{8,0},{1,9},{9,1},{2,10},{10,2},{3,11},{11,3},{4,12},{12,4},... | collective-permute-start | bytes 2359304 | tf_op jit(solution)/shard_map/ppermute | solution.py:60
  28.1 18.9 %collective-permute-start.4 = (bf16[2,2,1536,64]{2,3,1,0:T(8,128)(2,1)}, bf16[2,2,1536,64]{2,3,1,0:T(8,128)(2,1)}, u32[]{:S(2)}, u32[]{:S(2)}) collective-permute-start(bf16[2,2,1536,64]{2,3,1,0:T(8,128)(2,1)} %param.20), channel_id=1, source_target_pairs={{0,4},{4,0},{1,5},{5,1},{2,6},{6,2},{3,7},{7,3},{8,12},{12,8},{9,1... | collective-permute-start | bytes 2359304 | tf_op jit(solution)/shard_map/ppermute | solution.py:61
  46.2 2.6 collective-permute-start.6
  78.3 1.3 copy-start.9
  78.3 20.7 %collective-permute-start.3 = (bf16[192,6144]{1,0:T(8,128)(2,1)}, bf16[192,6144]{1,0:T(8,128)(2,1)}, u32[]{:S(2)}, u32[]{:S(2)}) collective-permute-start(bf16[192,6144]{1,0:T(8,128)(2,1)} %all-gather.5.cloned.1.call-done), channel_id=1, source_target_pairs={{0,4},{4,0},{1,5},{5,1},{2,6},{6,2},{3,7},{7,3},{8,12},{12,8},{9,1... | collective-permute-start | bytes 7077896 | tf_op jit(solution)/shard_map/ppermute | solution.py:91
  80.1 16.6 %copy-start.12 = (s32[384,2]{0,1:T(2,128)S(1)}, s32[384,2]{0,1:T(2,128)}, u32[]{:S(2)}) copy-start(s32[384,2]{0,1:T(2,128)} %param.13) | copy-start | bytes 9220
  96.6 1.3 collective-permute-start.7
  98.7 2.8 copy-start.10
  98.9 16.2 %copy-start.6 = (f32[3,128,2,1024]{3,1,0,2:T(8,128)}, f32[3,128,2,1024]{3,1,0,2:T(8,128)S(1)}, u32[]{:S(2)}) copy-start(f32[3,128,2,1024]{3,1,0,2:T(8,128)S(1)} %copy.20) | copy-start | bytes 9437188
  98.9 6.6 %copy-start.11 = (bf16[6144,8]{0,1:T(8,128)(2,1)S(1)}, bf16[6144,8]{0,1:T(8,128)(2,1)}, u32[]{:S(2)}) copy-start(bf16[6144,8]{0,1:T(8,128)(2,1)} %param.16) | copy-start | bytes 294916
  105.5 9.6 %copy-start.3 = (bf16[384,6144]{1,0:T(8,128)(2,1)}, bf16[384,6144]{1,0:T(8,128)(2,1)S(1)}, u32[]{:S(2)}) copy-start(bf16[384,6144]{1,0:T(8,128)(2,1)S(1)} %maximum_select_fusion) | copy-start | bytes 14155780
  124.1 125.9 %all-gather.7.cloned.1.call-start = ((), (), s32[]{:S(2)}) async-start(), calls=%async_computation.1 | async-start | bytes 3932160 | tf_op jit(solution)/shard_map/all_gather | solution.py:127
  124.4 11.1 %copy-start.4 = (bf16[384,6144]{1,0:T(8,128)(2,1)S(1)}, bf16[384,6144]{1,0:T(8,128)(2,1)}, u32[]{:S(2)}) copy-start(bf16[384,6144]{1,0:T(8,128)(2,1)} %copy-done.3) | copy-start | bytes 14155780
  124.4 11.1 %copy-start.7 = (f32[3,128,2,1024]{3,1,0,2:T(8,128)S(1)}, f32[3,128,2,1024]{3,1,0,2:T(8,128)}, u32[]{:S(2)}) copy-start(f32[3,128,2,1024]{3,1,0,2:T(8,128)} %copy-done.6) | copy-start | bytes 9437188
  259.4 1.4 copy-start.5
  260.9 2.9 %collective-permute-start.8 = (f32[2,96,1536]{2,1,0:T(8,128)S(1)}, f32[2,96,1536]{2,1,0:T(8,128)S(1)}, u32[]{:S(2)}, u32[]{:S(2)}) collective-permute-start(f32[2,96,1536]{2,1,0:T(8,128)S(1)} %select_bitcast_fusion), channel_id=1, source_target_pairs={{0,4},{4,0},{1,5},{5,1},{2,6},{6,2},{3,7},{7,3},{8,12},{12,8},{9,1... | collective-permute-start | bytes 3538952 | tf_op jit(solution)/shard_map/ppermute | solution.py:139
  263.8 12.0 %copy-start.1 = (bf16[8,2,64,1024]{3,2,1,0:T(8,128)(2,1)S(1)}, bf16[8,2,64,1024]{3,2,1,0:T(8,128)(2,1)}, u32[]{:S(2)}) copy-start(bf16[8,2,64,1024]{3,2,1,0:T(8,128)(2,1)} %param.21) | copy-start | bytes 6291460
  265.9 9.1 %collective-permute-start.9 = (bf16[96,1536]{1,0:T(8,128)(2,1)S(1)}, bf16[96,1536]{1,0:T(8,128)(2,1)S(1)}, u32[]{:S(2)}, u32[]{:S(2)}) collective-permute-start(bf16[96,1536]{1,0:T(8,128)(2,1)S(1)} %fusion.42), channel_id=1, source_target_pairs={{0,8},{8,0},{1,9},{9,1},{2,10},{10,2},{3,11},{11,3},{4,12},{12,4},... | collective-permute-start | bytes 884744 | tf_op jit(solution)/shard_map/ppermute | solution.py:144
Sparse Core Ops, SparseCore 0:
  26.3 51.9 all-gather.4
  124.3 62.0 all-gather.8
  187.9 62.1 all-gather.6
where the time goes:
time: 283 us; the launch traced here: 282 us
  waiting for transfers between devices  160 us (57%)
  matrix products  59.1 us (21%)
  blocking collectives  15.9 us (6%)
  other arithmetic  15.3 us (5%)
  between operations  13.5 us (5%)
  local copies, waits for them, and re-layouts  11.5 us (4%)
  starting transfers between devices  6.73 us (2%)
    all_gather x2, waiting for transfers between devices, per_device(): gathered = lax.all_gather(hidden, 'expert', axis=1, tiled=True)  95.4 us
    all_gather x1, waiting for transfers between devices, per_device(): mine = lax.all_gather(mine_q, 'expert', axis=1, tiled=True)  23.7 us
    dot_general x2, matrix products, per_device(): jnp.dot(gathered, down_weight[expert_number], preferred_element_type=jnp....  19.3 us
    dot_general x2, matrix products, per_device(): jnp.dot(input_rows, gate_weight[expert_number], preferred_element_type=jn...  19.2 us
    ppermute x1, waiting for transfers between devices, per_device(): from_chip = lax.ppermute(adapter_down_weight, 'wy', swap)  18.2 us
    dot_general x2, matrix products, per_device(): jnp.dot(input_rows, up_weight[expert_number], preferred_element_type=jnp....  18.1 us
    all_gather x1, blocking collectives, per_device(): lax.all_gather(rank_q, 'expert', axis=1, tiled=False).astype(jnp.float32)  15.9 us
    ppermute x1, waiting for transfers between devices, per_device(): slot_chip = lax.ppermute(prompts, 'wy', pair)  9.32 us
  transfers between devices with their start and end apart: 13, of which 10 were waited for; matrix products, arithmetic and copies ran while one was open for 14% of the time, Pallas kernels for 0%

commit v1 on v0

--- a/solution.py
+++ b/solution.py
@@ -8,6 +8,16 @@
 ADAPTER_SCALE = 0.5
 WIDE = ("wy", "wc")
 GROUP = ("wy", "wc", "expert")
+
+
+def pass_along(x, name, dim):
+    size = lax.axis_size(name)
+    held, tiles = (x, [x])
+    for _ in range(size - 1):
+        held = lax.ppermute(held, name, [(i, (i + 1) % size) for i in range(size)])
+        tiles.insert(0, held)
+    line = jnp.concatenate(tiles, axis=dim)
+    return jnp.roll(line, (lax.axis_index(name) + 1) * x.shape[dim], axis=dim)
 
 
 def per_device(
@@ -124,7 +134,7 @@
         hidden = (weight[:, expert_number, None] * jax.nn.silu(gate_pre) * up_value).astype(
             jnp.bfloat16
         )
-        gathered = lax.all_gather(hidden, "expert", axis=1, tiled=True)
+        gathered = pass_along(hidden, "expert", 1)
         part = jnp.dot(gathered, down_weight[expert_number], preferred_element_type=jnp.float32)
         running = part if running is None else running + part
     return reduce_rows(running, core, cores).astype(jnp.bfloat16)

time: 283 us -> 274 us (0.968)
  waiting for transfers between devices: 160 us -> 148 us
    all_gather x2 -> x0, waiting for transfers between devices: 95.4 us -> none  [per_device(): gathered = lax.all_gather(hidden, 'expert', axis=1, tiled=True)]
    ppermute x0 -> x6, waiting for transfers between devices: none -> 83.2 us  [pass_along(): held = lax.ppermute(held, name, [(i, (i + 1) % size) for i in range(size)])]
    dot_general x2, matrix products: 19.3 us -> 25.4 us  [per_device(): jnp.dot(gathered, down_weight[expert_number], preferred_element_type=jnp....]
    dot_general x2, matrix products: 19.2 us -> 16.1 us  [per_device(): jnp.dot(input_rows, gate_weight[expert_number], preferred_element_type=jn...]
  transfers between devices with their start and end apart: 13 -> 17, of which waited for: 10 -> 14; matrix products, arithmetic and copies ran while one was open for 14% -> 12% of each run, Pallas kernels for 0% -> 0%
where the time goes in v1:
time: 274 us; the launch traced here: 273 us
  waiting for transfers between devices  148 us (54%)
  matrix products  61.8 us (23%)
  other arithmetic  16.2 us (6%)
  blocking collectives  16.2 us (6%)
  between operations  13.7 us (5%)
  local copies, waits for them, and re-layouts  9.22 us (3%)
  starting transfers between devices  7.79 us (3%)
    ppermute x6, waiting for transfers between devices, pass_along(): held = lax.ppermute(held, name, [(i, (i + 1) % size) for i in range(size)])  83.2 us
    dot_general x2, matrix products, per_device(): jnp.dot(gathered, down_weight[expert_number], preferred_element_type=jnp....  25.4 us
    all_gather x1, waiting for transfers between devices, per_device(): mine = lax.all_gather(mine_q, 'expert', axis=1, tiled=True)  23.7 us
    ppermute x1, waiting for transfers between devices, per_device(): from_chip = lax.ppermute(adapter_down_weight, 'wy', swap)  18.2 us
    dot_general x2, matrix products, per_device(): jnp.dot(input_rows, up_weight[expert_number], preferred_element_type=jnp....  16.5 us
    all_gather x1, blocking collectives, per_device(): lax.all_gather(rank_q, 'expert', axis=1, tiled=False).astype(jnp.float32)  16.2 us
    dot_general x2, matrix products, per_device(): jnp.dot(input_rows, gate_weight[expert_number], preferred_element_type=jn...  16.1 us
    ppermute x1, waiting for transfers between devices, per_device(): slot_chip = lax.ppermute(prompts, 'wy', pair)  9.32 us
  transfers between devices with their start and end apart: 17, of which 14 were waited for; matrix products, arithmetic and copies ran while one was open for 12% of the time, Pallas kernels for 0%

profile of v1, /device:TPU:0, one launch (start us, length us, event | category | flops | bytes accessed | tf_op | source)
XLA Modules:
  0.0 273.3 jit_solution(14417550357303377456)
XLA Ops:
  6.5 3.0 %collective-permute-start.1 = (bf16[1,128,1536]{2,1,0:T(8,128)(2,1)}, bf16[1,128,1536]{2,1,0:T(8,128)(2,1)S(1)}, u32[]{:S(2)}, u32[]{:S(2)}) collective-permute-start(bf16[1,128,1536]{2,1,0:T(8,128)(2,1)} %param.13), channel_id=1, source_target_pairs={{0,8},{8,0},{1,9},{9,1},{2,10},{10,2},{3,11},{11,3},{4,12},{12,4},... | collective-permute-start | bytes 1179656 | tf_op jit(solution)/shard_map/ppermute | solution.py:52
  9.5 9.3 %collective-permute-done.1 = bf16[1,128,1536]{2,1,0:T(8,128)(2,1)S(1)} collective-permute-done((bf16[1,128,1536]{2,1,0:T(8,128)(2,1)}, bf16[1,128,1536]{2,1,0:T(8,128)(2,1)S(1)}, u32[]{:S(2)}, u32[]{:S(2)}) %collective-permute-start.1) | collective-permute-done | bytes 393248 | tf_op jit(solution)/shard_map/ppermute | solution.py:52
  18.8 0.7 compare_and_fusion.2
  19.7 0.9 collective-permute-done.2
  20.6 2.4 pad_maximum_fusion.1
  22.9 2.0 gather_fusion
  25.0 1.1 dynamic-slice_select_fusion
  26.1 1.8 collective-permute-start.5
  27.9 18.2 %collective-permute-done.5 = bf16[2,2,1536,64]{2,3,1,0:T(8,128)(2,1)} collective-permute-done((bf16[2,2,1536,64]{2,3,1,0:T(8,128)(2,1)}, bf16[2,2,1536,64]{2,3,1,0:T(8,128)(2,1)}, u32[]{:S(2)}, u32[]{:S(2)}) %collective-permute-start.5) | collective-permute-done | bytes 786464 | tf_op jit(solution)/shard_map/ppermute | solution.py:70
  46.1 0.6 gather_fusion.2
  46.8 1.9 collective-permute-done.6
  48.7 3.2 %pad_maximum_fusion = bf16[4,2,2,1536,64]{3,4,2,1,0:T(8,128)(2,1)} fusion(bf16[1,2,2,1536,64]{3,4,2,1,0:T(8,128)(2,1)} %bitcast.9, bf16[1,2,2,1536,64]{3,4,2,1,0:T(8,128)(2,1)} %bitcast.8, bf16[1,2,2,1536,64]{3,4,2,1,0:T(8,128)(2,1)} %bitcast.7, bf16[1,2,2,1536,64]{3,4,2,1,0:T(8,128)(2,1)} %bitcast.117), kind=kLoop, calls=%fused_computation.53 | loop fusion | flops 4718592 | bytes 6291456 | tf_op jit(solution)/shard_map/stack | solution.py:73
  52.0 2.5 gather_fusion.3
  54.5 23.7 %all-gather.3.cloned.1.call-done = bf16[192,6144]{1,0:T(8,128)(2,1)} async-done(((bf16[192,1536]{1,0:T(8,128)(2,1)}), bf16[192,6144]{1,0:T(8,128)(2,1)}) %all-gather.3.cloned.1.call-update) | async-done | bytes 2359312 | tf_op jit(solution)/shard_map/all_gather | solution.py:93
  78.2 0.2 broadcast_select_fusion
  78.4 1.8 fusion.53
  80.2 0.1 copy.18
  80.4 0.2 fusion.64
  80.6 16.2 %all-gather = bf16[192,1024]{0,1:T(8,128)(2,1)S(1)} all-gather(bf16[192,256]{0,1:T(8,128)(2,1)S(1)} %fusion.64), channel_id=2, replica_groups=mesh['groups'=2,'wy'=2,'wc'=2,'expert'=4] {'expert'}, dimensions={1}, use_global_device_ids=true | all-gather | bytes 491520 | tf_op jit(solution)/shard_map/all_gather | solution.py:98
  96.8 0.1 bitcast_convert_fusion
  97.1 0.6 gather_fusion.1
  97.7 0.6 collective-permute-done.7
  98.3 0.1 maximum_select_fusion.1
  98.4 0.6 convolution_bitcast_fusion
  99.1 0.2 copy.20
  99.3 1.4 copy-done.5
  100.7 4.0 %maximum_select_fusion = bf16[384,6144]{1,0:T(8,128)(2,1)S(1)} fusion(bf16[192,6144]{1,0:T(8,128)(2,1)} %collective-permute-done.3, bf16[192,6144]{1,0:T(8,128)(2,1)S(1)} %copy-done.5, pred[]{:T(512)S(6)} %eq.16), kind=kLoop, calls=%fused_computation.38 | loop fusion | flops 21233664 | bytes 9437185 | tf_op jit(solution)/shard_map/jit(_where)/select_n | solution.py:103
  104.8 8.1 %fusion.4 = f32[384,1024]{1,0:T(8,128)S(1)} fusion(bf16[384,6144]{1,0:T(8,128)(2,1)S(1)} %maximum_select_fusion, bf16[2,6144,1024]{2,1,0:T(8,128)(2,1)} %param.19), kind=kOutput, calls=%fused_computation.8 | convolution fusion | flops 4831838208 | bytes 18874368 | tf_op jit(solution)/shard_map/dot_general | solution.py:127
  112.9 8.0 %fusion.10 = f32[384,1024]{1,0:T(8,128)S(1)} fusion(bf16[384,6144]{1,0:T(8,128)(2,1)S(1)} %maximum_select_fusion, bf16[2,6144,1024]{2,1,0:T(8,128)(2,1)} %param.19), kind=kOutput, calls=%fused_computation.14 | convolution fusion | flops 4831838208 | bytes 18874368 | tf_op jit(solution)/shard_map/dot_general | solution.py:127
  120.9 1.3 fusion.77
  122.4 8.2 %fusion.44 = bf16[384,1024]{1,0:T(8,128)(2,1)S(1)} fusion(f32[384,2,1024]{2,0,1:T(8,128)S(1)} %bitcast.112, f32[384,1024]{1,0:T(8,128)S(1)} %fusion.4, bf16[384,6144]{1,0:T(8,128)(2,1)S(1)} %maximum_select_fusion, bf16[2,6144,1024]{2,1,0:T(8,128)(2,1)} %param.20, f32[384]{0:T(512)S(1)} %get-tuple-element.9), kind=kOutput, calls=%fused_computation.60 | convolution fusion | flops 4835377152 | bytes 21235200 | tf_op jit(solution)/shard_map/dot_general | solution.py:131
  130.6 8.3 %fusion.48 = bf16[384,1024]{1,0:T(8,128)(2,1)S(1)} fusion(f32[384,2,1024]{2,0,1:T(8,128)S(1)} %bitcast.113, f32[384,1024]{1,0:T(8,128)S(1)} %fusion.10, bf16[384,6144]{1,0:T(8,128)(2,1)S(1)} %maximum_select_fusion, bf16[2,6144,1024]{2,1,0:T(8,128)(2,1)} %param.20, f32[384]{0:T(512)S(1)} %get-tuple-element.8), kind=kOutput, calls=%fused_computation.65 | convolution fusion | flops 4835377152 | bytes 21235200 | tf_op jit(solution)/shard_map/dot_general | solution.py:131
  139.0 1.3 collective-permute-start.8
  140.3 12.5 %collective-permute-done.11 = bf16[384,1024]{1,0:T(8,128)(2,1)S(1)} collective-permute-done((bf16[384,1024]{1,0:T(8,128)(2,1)S(1)}, bf16[384,1024]{1,0:T(8,128)(2,1)S(1)}, u32[]{:S(2)}, u32[]{:S(2)}) %collective-permute-start.11) | collective-permute-done | bytes 786464 | tf_op jit(solution)/shard_map/ppermute | solution.py:17
  152.8 17.0 %collective-permute-done.8 = bf16[384,1024]{1,0:T(8,128)(2,1)} collective-permute-done((bf16[384,1024]{1,0:T(8,128)(2,1)S(1)}, bf16[384,1024]{1,0:T(8,128)(2,1)}, u32[]{:S(2)}, u32[]{:S(2)}) %collective-permute-start.8) | collective-permute-done | bytes 786464 | tf_op jit(solution)/shard_map/ppermute | solution.py:17
  169.8 16.8 %collective-permute-done.12 = bf16[384,1024]{1,0:T(8,128)(2,1)} collective-permute-done((bf16[384,1024]{1,0:T(8,128)(2,1)S(1)}, bf16[384,1024]{1,0:T(8,128)(2,1)}, u32[]{:S(2)}, u32[]{:S(2)}) %collective-permute-start.12) | collective-permute-done | bytes 786464 | tf_op jit(solution)/shard_map/ppermute | solution.py:17
  186.6 16.8 %collective-permute-done.9 = bf16[384,1024]{1,0:T(8,128)(2,1)} collective-permute-done((bf16[384,1024]{1,0:T(8,128)(2,1)}, bf16[384,1024]{1,0:T(8,128)(2,1)}, u32[]{:S(2)}, u32[]{:S(2)}) %collective-permute-start.9) | collective-permute-done | bytes 786464 | tf_op jit(solution)/shard_map/ppermute | solution.py:17
  203.5 16.8 %collective-permute-done.13 = bf16[384,1024]{1,0:T(8,128)(2,1)} collective-permute-done((bf16[384,1024]{1,0:T(8,128)(2,1)}, bf16[384,1024]{1,0:T(8,128)(2,1)}, u32[]{:S(2)}, u32[]{:S(2)}) %collective-permute-start.13) | collective-permute-done | bytes 786464 | tf_op jit(solution)/shard_map/ppermute | solution.py:17
  220.3 12.8 %fusion = f32[384,1536]{1,0:T(8,128)S(1)} fusion(bf16[2,4096,1536]{2,1,0:T(8,128)(2,1)} %param.21, s32[]{:T(128)S(6)} %select_n.163, bf16[384,1024]{1,0:T(8,128)(2,1)} %collective-permute-done.13, bf16[384,1024]{1,0:T(8,128)(2,1)} %collective-permute-done.12, bf16[384,1024]{1,0:T(8,128)(2,1)S(1)} %collective-permute-done.11, bf16[384,1024]{1,0:T(8,128)(2,1)S(1)} %fusion.44), kind=kOutput, calls=%fused_computation.4 | convolution fusion | flops 4857004032 | bytes 18087940 | tf_op jit(solution)/shard_map/dot_general | solution.py:138
  233.1 3.2 %collective-permute-done.10 = bf16[384,1024]{1,0:T(8,128)(2,1)S(1)} collective-permute-done((bf16[384,1024]{1,0:T(8,128)(2,1)}, bf16[384,1024]{1,0:T(8,128)(2,1)S(1)}, u32[]{:S(2)}, u32[]{:S(2)}) %collective-permute-start.10) | collective-permute-done | bytes 786464 | tf_op jit(solution)/shard_map/ppermute | solution.py:17
  236.3 12.6 %fusion.36 = f32[384,1536]{1,0:T(8,128)S(1)} fusion(f32[384,1536]{1,0:T(8,128)S(1)} %fusion, bf16[2,4096,1536]{2,1,0:T(8,128)(2,1)} %param.21, s32[]{:T(128)S(6)} %select_n.163, bf16[384,1024]{1,0:T(8,128)(2,1)S(1)} %collective-permute-done.10, bf16[384,1024]{1,0:T(8,128)(2,1)} %collective-permute-done.9, bf16[384,1024]{1,0:T(8,128)(2,1)} %collective-permute-done.8, ...), kind=kOutput, calls=%fused_computation.54 | convolution fusion | flops 4857593856 | bytes 20447236 | tf_op jit(solution)/shard_map/dot_general | solution.py:138
  248.9 1.4 copy-done.3
  250.4 1.2 select_bitcast_fusion
  251.5 3.1 %collective-permute-done.14 = f32[2,96,1536]{2,1,0:T(8,128)S(1)} collective-permute-done((f32[2,96,1536]{2,1,0:T(8,128)}, f32[2,96,1536]{2,1,0:T(8,128)S(1)}, u32[]{:S(2)}, u32[]{:S(2)}) %collective-permute-start.14) | collective-permute-done | bytes 1179680 | tf_op jit(solution)/shard_map/ppermute | solution.py:149
  254.6 1.9 bitcast_add_fusion
  256.5 1.5 collective-permute-start.15
  258.0 7.6 %collective-permute-done.15 = bf16[96,1536]{1,0:T(8,128)(2,1)S(1)} collective-permute-done((bf16[96,1536]{1,0:T(8,128)(2,1)S(1)}, bf16[96,1536]{1,0:T(8,128)(2,1)S(1)}, u32[]{:S(2)}, u32[]{:S(2)}) %collective-permute-start.15) | collective-permute-done | bytes 294944 | tf_op jit(solution)/shard_map/ppermute | solution.py:154
  265.6 0.8 fusion.58
  (49 shorter events, 0.7 us)
Async XLA Ops:
  6.5 90.5 %copy-start = (bf16[8,2,64,1024]{3,2,1,0:T(8,128)(2,1)S(1)}, bf16[8,2,64,1024]{3,2,1,0:T(8,128)(2,1)}, u32[]{:S(2)}) copy-start(bf16[8,2,64,1024]{3,2,1,0:T(8,128)(2,1)} %param.23) | copy-start | bytes 6291460
  6.5 71.7 %all-gather.3.cloned.1.call-start = ((), (), s32[]{:S(2)}) async-start(), calls=%async_computation | async-start | bytes 2949120 | tf_op jit(solution)/shard_map/all_gather | solution.py:93
  6.5 12.3 %collective-permute-start.1 = (bf16[1,128,1536]{2,1,0:T(8,128)(2,1)}, bf16[1,128,1536]{2,1,0:T(8,128)(2,1)S(1)}, u32[]{:S(2)}, u32[]{:S(2)}) collective-permute-start(bf16[1,128,1536]{2,1,0:T(8,128)(2,1)} %param.13), channel_id=1, source_target_pairs={{0,8},{8,0},{1,9},{9,1},{2,10},{10,2},{3,11},{11,3},{4,12},{12,4},... | collective-permute-start | bytes 1179656 | tf_op jit(solution)/shard_map/ppermute | solution.py:52
  9.5 10.2 %collective-permute-start = (bf16[1,128,1536]{2,1,0:T(8,128)(2,1)}, bf16[1,128,1536]{2,1,0:T(8,128)(2,1)S(1)}, u32[]{:S(2)}, u32[]{:S(2)}) collective-permute-start(bf16[1,128,1536]{2,1,0:T(8,128)(2,1)} %param.13), channel_id=1, source_target_pairs={{0,4},{4,0},{1,5},{5,1},{2,6},{6,2},{3,7},{7,3},{8,12},{12,8},{9,1... | collective-permute-start | bytes 1179656 | tf_op jit(solution)/shard_map/ppermute | solution.py:53
  18.8 1.7 collective-permute-start.2
  19.7 26.4 %copy-start.8 = (s32[3]{0:T(128)S(1)}, s32[3]{0:T(128)}, u32[]{:S(2)}) copy-start(s32[3]{0:T(128)} %param.16) | copy-start | bytes 40
  19.7 26.5 %copy-start.2 = (s32[8]{0:T(128)S(1)}, s32[8]{0:T(128)}, u32[]{:S(2)}) copy-start(s32[8]{0:T(128)} %param.17) | copy-start | bytes 100
  24.9 27.0 %copy-start.4 = (bf16[3,128,1536]{2,1,0:T(8,128)(2,1)}, bf16[3,128,1536]{2,1,0:T(8,128)(2,1)S(1)}, u32[]{:S(2)}) copy-start(bf16[3,128,1536]{2,1,0:T(8,128)(2,1)S(1)} %gather_fusion) | copy-start | bytes 3538948
  26.1 20.0 %collective-permute-start.5 = (bf16[2,2,1536,64]{2,3,1,0:T(8,128)(2,1)}, bf16[2,2,1536,64]{2,3,1,0:T(8,128)(2,1)}, u32[]{:S(2)}, u32[]{:S(2)}) collective-permute-start(bf16[2,2,1536,64]{2,3,1,0:T(8,128)(2,1)} %param.22), channel_id=1, source_target_pairs={{0,8},{8,0},{1,9},{9,1},{2,10},{10,2},{3,11},{11,3},{4,12},{12,4},... | collective-permute-start | bytes 2359304 | tf_op jit(solution)/shard_map/ppermute | solution.py:70
  27.9 18.9 %collective-permute-start.4 = (bf16[2,2,1536,64]{2,3,1,0:T(8,128)(2,1)}, bf16[2,2,1536,64]{2,3,1,0:T(8,128)(2,1)}, u32[]{:S(2)}, u32[]{:S(2)}) collective-permute-start(bf16[2,2,1536,64]{2,3,1,0:T(8,128)(2,1)} %param.22), channel_id=1, source_target_pairs={{0,4},{4,0},{1,5},{5,1},{2,6},{6,2},{3,7},{7,3},{8,12},{12,8},{9,1... | collective-permute-start | bytes 2359304 | tf_op jit(solution)/shard_map/ppermute | solution.py:71
  46.1 2.6 collective-permute-start.6
  78.2 21.1 %collective-permute-start.3 = (bf16[192,6144]{1,0:T(8,128)(2,1)}, bf16[192,6144]{1,0:T(8,128)(2,1)}, u32[]{:S(2)}, u32[]{:S(2)}) collective-permute-start(bf16[192,6144]{1,0:T(8,128)(2,1)} %all-gather.3.cloned.1.call-done), channel_id=1, source_target_pairs={{0,4},{4,0},{1,5},{5,1},{2,6},{6,2},{3,7},{7,3},{8,12},{12,8},{9,1... | collective-permute-start | bytes 7077896 | tf_op jit(solution)/shard_map/ppermute | solution.py:101
  80.2 16.8 %copy-start.7 = (s32[384,2]{0,1:T(2,128)S(1)}, s32[384,2]{0,1:T(2,128)}, u32[]{:S(2)}) copy-start(s32[384,2]{0,1:T(2,128)} %param.15) | copy-start | bytes 9220
  97.0 1.3 collective-permute-start.7
  99.1 1.7 copy-start.5
  112.9 8.1 %copy-start.6 = (bf16[6144,8]{0,1:T(8,128)(2,1)S(1)}, bf16[6144,8]{0,1:T(8,128)(2,1)}, u32[]{:S(2)}) copy-start(bf16[6144,8]{0,1:T(8,128)(2,1)} %param.18) | copy-start | bytes 294916
  130.6 22.2 %collective-permute-start.11 = (bf16[384,1024]{1,0:T(8,128)(2,1)S(1)}, bf16[384,1024]{1,0:T(8,128)(2,1)S(1)}, u32[]{:S(2)}, u32[]{:S(2)}) collective-permute-start(bf16[384,1024]{1,0:T(8,128)(2,1)S(1)} %fusion.44), channel_id=1, source_target_pairs={{0,1},{1,2},{2,3},{3,0},{4,5},{5,6},{6,7},{7,4},{8,9},{9,10},{10,1... | collective-permute-start | bytes 2359304 | tf_op jit(solution)/shard_map/ppermute | solution.py:17
  139.0 30.8 %collective-permute-start.8 = (bf16[384,1024]{1,0:T(8,128)(2,1)S(1)}, bf16[384,1024]{1,0:T(8,128)(2,1)}, u32[]{:S(2)}, u32[]{:S(2)}) collective-permute-start(bf16[384,1024]{1,0:T(8,128)(2,1)S(1)} %fusion.48), channel_id=1, source_target_pairs={{0,1},{1,2},{2,3},{3,0},{4,5},{5,6},{6,7},{7,4},{8,9},{9,10},{10,1... | collective-permute-start | bytes 2359304 | tf_op jit(solution)/shard_map/ppermute | solution.py:17
  152.8 33.8 %collective-permute-start.12 = (bf16[384,1024]{1,0:T(8,128)(2,1)S(1)}, bf16[384,1024]{1,0:T(8,128)(2,1)}, u32[]{:S(2)}, u32[]{:S(2)}) collective-permute-start(bf16[384,1024]{1,0:T(8,128)(2,1)S(1)} %collective-permute-done.11), channel_id=1, source_target_pairs={{0,1},{1,2},{2,3},{3,0},{4,5},{5,6},{6,7},{7,4},{8,9},{9,10},{10,1... | collective-permute-start | bytes 2359304 | tf_op jit(solution)/shard_map/ppermute | solution.py:17
  169.8 33.7 %collective-permute-start.9 = (bf16[384,1024]{1,0:T(8,128)(2,1)}, bf16[384,1024]{1,0:T(8,128)(2,1)}, u32[]{:S(2)}, u32[]{:S(2)}) collective-permute-start(bf16[384,1024]{1,0:T(8,128)(2,1)} %collective-permute-done.8), channel_id=1, source_target_pairs={{0,1},{1,2},{2,3},{3,0},{4,5},{5,6},{6,7},{7,4},{8,9},{9,10},{10,1... | collective-permute-start | bytes 2359304 | tf_op jit(solution)/shard_map/ppermute | solution.py:17
  186.6 33.7 %collective-permute-start.13 = (bf16[384,1024]{1,0:T(8,128)(2,1)}, bf16[384,1024]{1,0:T(8,128)(2,1)}, u32[]{:S(2)}, u32[]{:S(2)}) collective-permute-start(bf16[384,1024]{1,0:T(8,128)(2,1)} %collective-permute-done.12), channel_id=1, source_target_pairs={{0,1},{1,2},{2,3},{3,0},{4,5},{5,6},{6,7},{7,4},{8,9},{9,10},{10,1... | collective-permute-start | bytes 2359304 | tf_op jit(solution)/shard_map/ppermute | solution.py:17
  203.5 32.8 %collective-permute-start.10 = (bf16[384,1024]{1,0:T(8,128)(2,1)}, bf16[384,1024]{1,0:T(8,128)(2,1)S(1)}, u32[]{:S(2)}, u32[]{:S(2)}) collective-permute-start(bf16[384,1024]{1,0:T(8,128)(2,1)} %collective-permute-done.9), channel_id=1, source_target_pairs={{0,1},{1,2},{2,3},{3,0},{4,5},{5,6},{6,7},{7,4},{8,9},{9,10},{10,1... | collective-permute-start | bytes 2359304 | tf_op jit(solution)/shard_map/ppermute | solution.py:17
  248.9 1.4 copy-start.3
  251.5 3.1 %collective-permute-start.14 = (f32[2,96,1536]{2,1,0:T(8,128)}, f32[2,96,1536]{2,1,0:T(8,128)S(1)}, u32[]{:S(2)}, u32[]{:S(2)}) collective-permute-start(f32[2,96,1536]{2,1,0:T(8,128)} %select_bitcast_fusion), channel_id=1, source_target_pairs={{0,4},{4,0},{1,5},{5,1},{2,6},{6,2},{3,7},{7,3},{8,12},{12,8},{9,1... | collective-permute-start | bytes 3538952 | tf_op jit(solution)/shard_map/ppermute | solution.py:149
  251.5 14.9 %copy-start.1 = (bf16[8,2,64,1024]{3,2,1,0:T(8,128)(2,1)S(1)}, bf16[8,2,64,1024]{3,2,1,0:T(8,128)(2,1)}, u32[]{:S(2)}) copy-start(bf16[8,2,64,1024]{3,2,1,0:T(8,128)(2,1)} %param.23) | copy-start | bytes 6291460
  256.5 9.1 %collective-permute-start.15 = (bf16[96,1536]{1,0:T(8,128)(2,1)S(1)}, bf16[96,1536]{1,0:T(8,128)(2,1)S(1)}, u32[]{:S(2)}, u32[]{:S(2)}) collective-permute-start(bf16[96,1536]{1,0:T(8,128)(2,1)S(1)} %fusion.62), channel_id=1, source_target_pairs={{0,8},{8,0},{1,9},{9,1},{2,10},{10,2},{3,11},{11,3},{4,12},{12,4},... | collective-permute-start | bytes 884744 | tf_op jit(solution)/shard_map/ppermute | solution.py:154
Sparse Core Ops, SparseCore 0:
  26.2 51.9 all-gather.2
